TPU v7x, 32 devices: a whole 2x2x4 slice. The times are simulated.
32 devices in a mesh: ang: 8 (over z, core), row: 4 (over y, x).
Axes of the slice: x: 2, y: 2, z: 4, core: 2. Of those that a mesh axis runs over, the one named last changes fastest.
Arguments:
- panels: bfloat16 [4, 32, 64, 2, 128], P('row', None, 'ang'), may hold values from -6 to 6
- panel_slot: int32 [4, 32], P('row'), may hold values from 0 to 15
- panel_cell: int32 [4, 32, 2], P('row'), may hold values from 0 to 15
- bloch_k: float32 [8, 2], replicated, may hold values from -3.140625 to 3.140625
- leaf_inverse: bfloat16 [8, 2, 8192, 256], P('ang', None, 'row'), may hold values from -0.25 to 0.25
- level_left: bfloat16 [8, 3, 2, 32, 8192], P('ang', None, None, None, 'row'), may hold values from -0.75 to 0.75
- level_right: bfloat16 [8, 3, 2, 32, 8192], P('ang', None, None, None, 'row'), may hold values from -0.125 to 0.125
- block_left: bfloat16 [8, 2, 32, 8192], P('ang', None, None, 'row'), may hold values from -0.75 to 0.75
- block_right: bfloat16 [8, 2, 32, 8192], P('ang', None, None, 'row'), may hold values from -0.09375 to 0.09375
- block_coupling: bfloat16 [8, 4, 2, 32, 128], P('ang', 'row'), may hold values from -0.375 to 0.375
- rank_count: int32 [8, 4], P('ang', 'row'), may hold values from 16 to 32
- quad_weight: float32 [8, 2], P('ang'), may hold values from -2 to 2
Outputs:
- response: float32 [64, 2, 8192], P('ang', None, 'row')
All inputs are finite; a program needn't handle non-finite values.
Results may differ from a plain program's by a relative error of at most 0.0045.
Values may be sent and summed in bfloat16 or wider, within the bound.
No kernel may reach another device: no remote copies, remote signals or barrier semaphores. Data moves between devices by JAX's collectives and lax.ppermute only.
A program may use at most 64 MiB of HBM per device.

v0:
```python
import jax
import jax.numpy as jnp
from jax import lax
from jax.sharding import PartitionSpec as P


def complex_product(form, left_real, left_imag, right_real, right_imag):

    def single(first, second):
        return jnp.einsum(form, first, second, preferred_element_type=jnp.float32)

    return (
        single(left_real, right_real) - single(left_imag, right_imag),
        single(left_real, right_imag) + single(left_imag, right_real),
    )


def assemble(phase_cosine, phase_sin, onehot, panel_group):
    coef_cos = phase_cosine[:, :, None] * onehot[None]
    coef_sin = phase_sin[:, :, None] * onehot[None]
    panel_real = panel_group[:, :, 0]
    panel_imag = panel_group[:, :, 1]

    def single(coefficient, entry_values):
        return jnp.einsum(
            "aqk,qsw->askw", coefficient, entry_values, preferred_element_type=jnp.float32
        )

    real_part = single(coef_cos, panel_real) + single(coef_sin, panel_imag)
    imag_part = single(coef_cos, panel_imag) - single(coef_sin, panel_real)
    stacked = jnp.stack([real_part, imag_part], 2)
    dims = stacked.shape
    return stacked.reshape(dims[0], dims[1], 2, dims[3] * dims[4]).astype(jnp.bfloat16)


def near_field(excite, leaf_block, right_factors, left_factors):
    source_count = excite.shape[0]
    row_count = excite.shape[2]
    leaf_width = leaf_block.shape[2]
    leaf_count = row_count // leaf_width
    rank_width = right_factors.shape[2]
    gathered_groups = excite.reshape(source_count, 2, leaf_count, leaf_width)
    real_part, imag_part = complex_product(
        "lwv,slv->slw",
        leaf_block[0].reshape(leaf_count, leaf_width, leaf_width),
        leaf_block[1].reshape(leaf_count, leaf_width, leaf_width),
        gathered_groups[:, 0],
        gathered_groups[:, 1],
    )
    real_part = real_part.reshape(source_count, row_count)
    imag_part = imag_part.reshape(source_count, row_count)
    for tree_level_index in range(right_factors.shape[0]):
        node_size = row_count // 2 ** (tree_level_index + 1)
        groups = row_count // node_size
        node_view = excite.reshape(source_count, 2, groups, node_size)
        right_real = right_factors[tree_level_index, 0].reshape(rank_width, groups, node_size)
        right_imag = right_factors[tree_level_index, 1].reshape(rank_width, groups, node_size)
        proj_real, proj_imag = complex_product(
            "rgm,sgm->sgr", right_real, right_imag, node_view[:, 0], node_view[:, 1]
        )
        projected = jnp.stack([proj_real, proj_imag], 1).astype(jnp.bfloat16)
        swapped = projected.reshape(source_count, 2, groups // 2, 2, rank_width)[
            :, :, :, ::-1
        ].reshape(source_count, 2, groups, rank_width)
        left_real = left_factors[tree_level_index, 0].reshape(rank_width, groups, node_size)
        left_imag = left_factors[tree_level_index, 1].reshape(rank_width, groups, node_size)
        add_real, add_imag = complex_product(
            "rgm,sgr->sgm", left_real, left_imag, swapped[:, 0], swapped[:, 1]
        )
        real_part = real_part + add_real.reshape(source_count, row_count)
        imag_part = imag_part + add_imag.reshape(source_count, row_count)
    return (real_part, imag_part)


def shards(
    panels,
    panel_slot,
    panel_cell,
    bloch_k,
    leaf_inverse,
    level_left,
    level_right,
    block_left,
    block_right,
    block_coupling,
    rank_count,
    quad_weight,
):
    local_angles = leaf_inverse.shape[0]
    row_count = leaf_inverse.shape[2]
    panel_width = panels.shape[4]
    slot_count = row_count // panel_width
    onehot = (panel_slot[0][:, None] == jnp.arange(slot_count, dtype=jnp.int32)[None, :]).astype(
        jnp.bfloat16
    )
    cell_float = panel_cell[0].astype(jnp.float32)
    own_wave = lax.dynamic_slice_in_dim(
        bloch_k, lax.axis_index("ang") * local_angles, local_angles, 0
    )
    theta = own_wave[:, 0:1] * cell_float[None, :, 0] + own_wave[:, 1:2] * cell_float[None, :, 1]
    own_cos = jnp.cos(theta).astype(jnp.bfloat16)
    own_sin = jnp.sin(theta).astype(jnp.bfloat16)
    excitation = assemble(
        own_cos, own_sin, onehot, lax.all_gather(panels, "ang", axis=2, tiled=True)[0]
    )
    rank_width = block_right.shape[2]
    rank_iota = jnp.arange(rank_width, dtype=jnp.int32)
    rank_masks = (rank_iota[None, :] < rank_count).astype(jnp.bfloat16)
    right_masked = block_right * rank_masks[:, None, :, None]
    left_masked = block_left * rank_masks[:, None, :, None]
    proj_real, proj_imag = complex_product(
        "arm,asm->asr",
        right_masked[:, 0],
        right_masked[:, 1],
        excitation[:, :, 0],
        excitation[:, :, 1],
    )
    projected = jnp.stack([proj_real, proj_imag], 2).astype(jnp.bfloat16)
    gathered = lax.all_gather(projected[:, None], "row", axis=1, tiled=True)
    number_of_blocks = gathered.shape[1]
    keep_other = (jnp.arange(number_of_blocks, dtype=jnp.int32) != lax.axis_index("row")).astype(
        jnp.bfloat16
    )
    gathered = gathered * keep_other[None, :, None, None, None]
    coupling = block_coupling[:, 0].reshape(
        local_angles, 2, rank_width, number_of_blocks, rank_width
    )
    coup_real, coup_imag = complex_product(
        "arjq,ajsq->asr", coupling[:, 0], coupling[:, 1], gathered[:, :, :, 0], gathered[:, :, :, 1]
    )
    coupled = jnp.stack([coup_real, coup_imag], 2).astype(jnp.bfloat16)
    excite_part = excitation[0]
    coupled_part = coupled[0]
    near_real, near_imag = near_field(excite_part, leaf_inverse[0], level_right[0], level_left[0])
    far_real, far_imag = complex_product(
        "rm,sr->sm", left_masked[0, 0], left_masked[0, 1], coupled_part[:, 0], coupled_part[:, 1]
    )
    field_real = near_real + far_real
    field_imag = near_imag + far_imag
    weight_real = quad_weight[0, 0]
    weight_imag = quad_weight[0, 1]
    summed = jnp.stack(
        [
            weight_real * field_real - weight_imag * field_imag,
            weight_real * field_imag + weight_imag * field_real,
        ],
        1,
    )
    return lax.psum_scatter(summed, "ang", scatter_dimension=0, tiled=True)


def solution(mesh):
    placed = (
        P("row", None, "ang", None, None),
        P("row", None),
        P("row", None, None),
        P(),
        P("ang", None, "row", None),
        P("ang", None, None, None, "row"),
        P("ang", None, None, None, "row"),
        P("ang", None, None, "row"),
        P("ang", None, None, "row"),
        P("ang", "row", None, None, None),
        P("ang", "row"),
        P("ang", None),
    )
    return jax.shard_map(
        shards, mesh=mesh, in_specs=placed, out_specs=P("ang", None, "row"), check_vma=False
    )
```

profile of v0, /device:TPU:0, one launch (start us, length us, event | category | flops | bytes accessed | tf_op | source)
XLA Modules:
  0.0 121.3 jit_solution(7901270127954322322)
XLA Ops:
  6.5 1.7 %copy.87 = bf16[1,32,8,2,128]{4,1,2,3,0:T(8,128)(2,1)} copy(bf16[1,32,8,2,128]{4,3,2,1,0:T(2,128)(2,1)} %param.12) | data formatting | bytes 262144 | tf_op args[0]
  8.3 0.7 convert_bitcast_fusion
  9.0 1.3 %fusion.122 = (bf16[1,1,32,2048]{3,2,1,0:T(8,128)(2,1)S(1)}, bf16[1,1,32,2048]{3,2,1,0:T(8,128)(2,1)S(1)}, bf16[1,1,32,2048]{3,2,1,0:T(8,128)(2,1)S(1)}, bf16[1,...) fusion(bf16[3,2,32,2048]{3,2,1,0:T(8,128)(2,1)} %bitcast.282), kind=kLoop, calls=%fused_computation.173 | loop fusion | bytes 1572864 | tf_op jit(solution)/shard_map/slice | solution.py:57
  11.1 0.7 fusion.125
  11.8 0.7 reshape_squeeze.55
  12.6 0.7 reshape_squeeze.56
  13.3 0.7 reshape_squeeze.57
  14.0 0.7 reshape_squeeze.58
  14.7 0.7 reshape_squeeze.51
  15.5 0.7 reshape_squeeze.52
  16.2 0.7 reshape_squeeze.53
  17.0 0.7 copy.151
  17.7 0.7 copy.152
  18.3 0.7 copy.153
  19.0 0.7 copy.154
  20.3 1.3 %convert_bitcast_fusion.1 = (bf16[32]{0:T(256)(128)(2,1)S(1)}, f32[32,1]{0,1:T(1,128)S(1)}) fusion(f32[32,2]{0,1:T(2,128)S(1)} %convert_bitcast_fusion, f32[]{:T(128)} %bitcast.4, f32[]{:T(128)} %bitcast.2), kind=kLoop, calls=%fused_computation.163 | loop fusion | flops 128 | bytes 456 | tf_op jit(solution)/shard_map/convert_element_type | solution.py:102
  21.7 0.7 fusion.123
  22.3 0.9 broadcast_multiply_fusion
  23.2 1.7 %fusion.120 = (bf16[1,1,2048,256]{3,2,1,0:T(8,128)(2,1)S(1)}, bf16[1,1,2048,256]{3,2,1,0:T(8,128)(2,1)S(1)}) fusion(bf16[1,2,2048,256]{3,2,1,0:T(8,128)(2,1)} %param.16), kind=kLoop, calls=%fused_computation.171 | loop fusion | bytes 4194304 | tf_op jit(solution)/shard_map/slice | solution.py:46
  24.9 8.9 %all-gather.2.cloned.1.call-done = bf16[1,32,64,2,128]{4,1,2,3,0:T(8,128)(2,1)} async-done(((bf16[1,32,8,2,128]{4,1,2,3,0:T(8,128)(2,1)}), bf16[1,32,64,2,128]{4,1,2,3,0:T(8,128)(2,1)}) %all-gather.2.cloned.1.call-update) | async-done | bytes 1048592 | tf_op jit(solution)/shard_map/all_gather | solution.py:104
  33.9 1.3 %fusion.28 = f32[16,64,128]{2,0,1:T(8,128)S(1)} fusion(bf16[32,64,2,128]{3,0,1,2:T(8,128)(2,1)} %bitcast.250, s32[32]{0:T(128)S(1)} %bitcast.298, bf16[32]{0:T(256)(128)(2,1)S(1)} %convert_bitcast_fusion.2), kind=kOutput, calls=%fused_computation.57 | convolution fusion | flops 8389632 | bytes 1048768 | tf_op jit(solution)/shard_map/aqk,qsw->askw/dot_general | solution.py:25
  35.2 2.1 %fusion.29 = f32[16,64,128]{2,0,1:T(8,128)} fusion(bf16[32,64,2,128]{3,0,1,2:T(8,128)(2,1)} %bitcast.251, s32[32]{0:T(128)S(1)} %bitcast.299, bf16[32]{0:T(256)(128)(2,1)S(1)} %convert_bitcast_fusion.2), kind=kOutput, calls=%fused_computation.58 | convolution fusion | flops 8389632 | bytes 1048768 | tf_op jit(solution)/shard_map/aqk,qsw->askw/dot_general | solution.py:25
  37.5 0.8 squeeze.94
  38.3 0.8 squeeze.88
  39.0 2.0 %fusion.11 = bf16[16,64,128]{2,0,1:T(8,128)(2,1)} fusion(f32[16,64,128]{2,0,1:T(8,128)} %fusion.29, bf16[32,64,2,128]{3,0,1,2:T(8,128)(2,1)S(1)} %bitcast.253, s32[32]{0:T(128)S(1)} %bitcast.301, bf16[32]{0:T(256)(128)(2,1)S(1)} %get-tuple-element.5), kind=kOutput, calls=%fused_computation.23 | convolution fusion | flops 8651776 | bytes 1311744 | tf_op jit(solution)/shard_map/aqk,qsw->askw/dot_general | solution.py:25
  41.0 1.1 squeeze.95
  42.1 1.7 %squeeze.90 = bf16[64,2,1024]{2,1,0:T(2,128)(2,1)} reshape(bf16[1,64,16,128]{3,2,1,0:T(8,128)(2,1)} %bitcast.260) | data formatting | bytes 524288 | tf_op jit(solution)/shard_map/squeeze | solution.py:59
  43.9 1.2 fusion.44
  45.1 1.1 fusion.40
  46.7 1.1 fusion.78
  47.8 1.1 fusion.80
  49.1 1.1 fusion.34
  50.2 1.1 fusion.30
  51.3 1.1 fusion.27
  52.4 1.1 fusion.26
  53.6 8.2 %all_gather.7 = bf16[1,4,64,2,32]{2,4,3,0,1:T(8,128)(2,1)S(1)} all-gather(bf16[1,1,64,2,32]{2,4,3,0,1:T(8,128)(2,1)S(1)} %maximum_bitcast_fusion), channel_id=1, replica_groups=mesh['ang'=8,'row'=4] {'row'}, dimensions={1}, use_global_device_ids=true | all-gather | bytes 40960 | tf_op jit(solution)/shard_map/all_gather | solution.py:119
  61.8 1.5 %convolution_bitcast_fusion = f32[64,32]{0,1:T(8,128)} fusion(bf16[1,1,32,4,32]{4,3,2,1,0:T(4,128)(2,1)} %get-tuple-element.24, bf16[1,4,64,2,32]{2,4,1,3,0:T(8,128)(2,1)S(1)} %copy_multiply_fusion), kind=kOutput, calls=%fused_computation.36 | convolution fusion | flops 524288 | bytes 49152 | tf_op jit(solution)/shard_map/arjq,ajsq->asr/dot_general | solution.py:10
  63.3 1.5 %convolution_bitcast_fusion.2 = f32[64,32]{0,1:T(8,128)} fusion(bf16[1,1,32,4,32]{4,3,2,1,0:T(4,128)(2,1)} %get-tuple-element.24, bf16[1,4,64,2,32]{2,4,1,3,0:T(8,128)(2,1)S(1)} %copy_multiply_fusion), kind=kOutput, calls=%fused_computation.38 | convolution fusion | flops 524288 | bytes 49152 | tf_op jit(solution)/shard_map/arjq,ajsq->asr/dot_general | solution.py:10
  64.9 1.1 fusion.60
  66.0 1.1 fusion.54
  67.6 1.1 fusion.70
  68.7 1.1 fusion.68
  69.8 1.2 %fusion.62 = f32[8,64,256]{2,1,0:T(8,128)} fusion(bf16[8,256,256]{2,1,0:T(8,128)(2,1)S(1)} %bitcast.246, bf16[64,8,256]{2,1,0:T(8,128)(2,1)S(1)} %squeeze.86), kind=kOutput, calls=%fused_computation.91 | convolution fusion | flops 67108864 | bytes 1835008 | tf_op jit(solution)/shard_map/lwv,slv->slw/dot_general | solution.py:10
  71.0 1.2 %fusion.52 = f32[8,64,256]{2,1,0:T(8,128)} fusion(bf16[8,256,256]{2,1,0:T(8,128)(2,1)S(1)} %bitcast.247, bf16[64,8,256]{2,1,0:T(8,128)(2,1)S(1)} %squeeze.87), kind=kOutput, calls=%fused_computation.81 | convolution fusion | flops 67108864 | bytes 1835008 | tf_op jit(solution)/shard_map/lwv,slv->slw/dot_general | solution.py:10
  78.9 1.7 %subtract_bitcast_fusion = (f32[64,1,2048]{2,0,1:T(8,128)S(1)}, f32[64,1,2048]{2,0,1:T(8,128)S(1)}) fusion(f32[64,2048]{1,0:T(8,128)S(1)} %fusion, f32[]{:T(128)} %bitcast.66, f32[]{:T(128)} %bitcast, f32[64,2048]{1,0:T(8,128)S(1)} %fusion.64, bf16[64,32]{0,1:T(8,128)(2,1)S(1)} %fusion.23, bf16[1,2,32,2048]{3,2,1,0:T(8,128)(2,1)S(1)} %copy-done.3, ...), kind=kOutput, calls=%fused_computation.56 | convolution fusion | flops 9830400 | bytes 4333576 | tf_op jit(solution)/shard_map/rm,sr->sm/dot_general | solution.py:10
  80.6 1.1 pad_maximum_fusion
  81.7 31.1 %reduce-scatter.2.cloned.1.call-done = f32[8,2,2048]{2,0,1:T(8,128)} async-done(((f32[64,2,2048]{2,0,1:T(8,128)}), f32[8,2,2048]{2,0,1:T(8,128)}) %reduce-scatter.2.cloned.1.call-update) | async-done | bytes 131088 | tf_op jit(solution)/shard_map/reduce_scatter | solution.py:149
  112.8 1.7 %copy.140 = f32[8,2,2048]{2,1,0:T(2,128)} copy(f32[8,2,2048]{2,0,1:T(8,128)} %reduce-scatter.2.cloned.1.call-done) | data formatting | bytes 262144 | tf_op jit(solution)/shard_map/reduce_scatter | solution.py:149
  (136 shorter events, 8.8 us)
Async XLA Ops:
  6.5 5.2 %copy-start = (f32[8,2]{0,1:T(2,128)S(1)}, f32[8,2]{0,1:T(2,128)}, u32[]{:S(2)}) copy-start(f32[8,2]{0,1:T(2,128)} %param.15) | copy-start | bytes 196
  6.5 3.7 %copy-start.18 = (bf16[1,3,2,32,2048]{4,3,2,1,0:T(8,128)(2,1)S(1)}, bf16[1,3,2,32,2048]{4,3,2,1,0:T(8,128)(2,1)}, u32[]{:S(2)}) copy-start(bf16[1,3,2,32,2048]{4,3,2,1,0:T(8,128)(2,1)} %param.17) | copy-start | bytes 2359300
  6.5 4.5 %copy-start.40 = (f32[1,2]{1,0:T(1,128)S(1)}, f32[1,2]{1,0:T(1,128)}, u32[]{:S(2)}) copy-start(f32[1,2]{1,0:T(1,128)} %param.23) | copy-start | bytes 28
  6.5 27.3 %all-gather.2.cloned.1.call-start = ((), (), s32[]{:S(2)}) async-start(), calls=%async_computation.1 | async-start | bytes 1179648 | tf_op jit(solution)/shard_map/all_gather | solution.py:104
  8.2 104.6 %reduce-scatter.2.cloned.1.call-start = ((), (), s32[]{:S(2)}) async-start(), calls=%async_computation.2 | async-start | bytes 1179648 | tf_op jit(solution)/shard_map/reduce_scatter | solution.py:149
  10.2 9.4 %copy-start.38 = (bf16[1,1,2,32,128]{4,3,2,1,0:T(8,128)(2,1)S(1)}, bf16[1,1,2,32,128]{4,3,2,1,0:T(8,128)(2,1)}, u32[]{:S(2)}) copy-start(bf16[1,1,2,32,128]{4,3,2,1,0:T(8,128)(2,1)} %param.21) | copy-start | bytes 49156
  10.3 12.0 %copy-start.29 = (bf16[1,2,32,2048]{3,2,1,0:T(8,128)(2,1)S(1)}, bf16[1,2,32,2048]{3,2,1,0:T(8,128)(2,1)}, u32[]{:S(2)}) copy-start(bf16[1,2,32,2048]{3,2,1,0:T(8,128)(2,1)} %param.19) | copy-start | bytes 786436
  10.3 12.0 %copy-start.30 = (bf16[1,2,32,2048]{3,2,1,0:T(8,128)(2,1)S(1)}, bf16[1,2,32,2048]{3,2,1,0:T(8,128)(2,1)}, u32[]{:S(2)}) copy-start(bf16[1,2,32,2048]{3,2,1,0:T(8,128)(2,1)} %param.20) | copy-start | bytes 786436
  23.2 10.6 %copy-start.39 = (s32[1,32]{1,0:T(1,128)S(1)}, s32[1,32]{1,0:T(1,128)}, u32[]{:S(2)}) copy-start(s32[1,32]{1,0:T(1,128)} %param.13) | copy-start | bytes 388
  33.8 3.4 %copy-start.1 = (bf16[1,32,64,2,128]{4,1,2,3,0:T(8,128)(2,1)S(1)}, bf16[1,32,64,2,128]{4,1,2,3,0:T(8,128)(2,1)}, u32[]{:S(2)}) copy-start(bf16[1,32,64,2,128]{4,1,2,3,0:T(8,128)(2,1)} %all-gather.2.cloned.1.call-done) | copy-start | bytes 3145732
  41.0 5.2 %copy-start.35 = (bf16[32,4,512]{2,1,0:T(4,128)(2,1)S(1)}, bf16[32,4,512]{2,1,0:T(4,128)(2,1)}, u32[]{:S(2)}) copy-start(bf16[32,4,512]{2,1,0:T(4,128)(2,1)} %reshape_squeeze.56) | copy-start | bytes 393220
  41.0 5.4 %copy-start.28 = (bf16[64,4,512]{2,1,0:T(4,128)(2,1)S(1)}, bf16[64,4,512]{2,1,0:T(4,128)(2,1)}, u32[]{:S(2)}) copy-start(bf16[64,4,512]{2,1,0:T(4,128)(2,1)} %squeeze.94) | copy-start | bytes 786436
  41.0 5.7 %copy-start.15 = (bf16[32,4,512]{2,1,0:T(4,128)(2,1)S(1)}, bf16[32,4,512]{2,1,0:T(4,128)(2,1)}, u32[]{:S(2)}) copy-start(bf16[32,4,512]{2,1,0:T(4,128)(2,1)} %reshape_squeeze.57) | copy-start | bytes 393220
  43.9 5.1 %copy-start.2 = (bf16[16,64,128]{2,0,1:T(8,128)(2,1)S(1)}, bf16[16,64,128]{2,0,1:T(8,128)(2,1)}, u32[]{:S(2)}) copy-start(bf16[16,64,128]{2,0,1:T(8,128)(2,1)} %fusion.11) | copy-start | bytes 786436
  46.7 2.2 %copy-start.21 = (bf16[64,2,2,2,32]{0,4,3,2,1:T(8,128)(2,1)}, bf16[64,2,2,2,32]{0,4,3,2,1:T(8,128)(2,1)S(1)}, u32[]{:S(2)}) copy-start(bf16[64,2,2,2,32]{0,4,3,2,1:T(8,128)(2,1)S(1)} %rev.7) | copy-start | bytes 98308
  48.9 18.2 %copy-start.14 = (bf16[4,8,8,256]{3,2,1,0:T(8,128)(2,1)S(1)}, bf16[4,8,8,256]{3,2,1,0:T(8,128)(2,1)}, u32[]{:S(2)}) copy-start(bf16[4,8,8,256]{3,2,1,0:T(8,128)(2,1)} %copy.152) | copy-start | bytes 393220
  51.3 16.4 %copy-start.13 = (bf16[4,8,8,256]{3,2,1,0:T(8,128)(2,1)S(1)}, bf16[4,8,8,256]{3,2,1,0:T(8,128)(2,1)}, u32[]{:S(2)}) copy-start(bf16[4,8,8,256]{3,2,1,0:T(8,128)(2,1)} %copy.153) | copy-start | bytes 393220
  61.8 8.0 %copy-start.19 = (bf16[1,4,64,2,32]{2,4,1,3,0:T(8,128)(2,1)}, bf16[1,4,64,2,32]{2,4,1,3,0:T(8,128)(2,1)S(1)}, u32[]{:S(2)}) copy-start(bf16[1,4,64,2,32]{2,4,1,3,0:T(8,128)(2,1)S(1)} %copy_multiply_fusion) | copy-start | bytes 98308
  67.6 4.7 %copy-start.16 = (bf16[64,2,4,2,32]{0,4,3,2,1:T(8,128)(2,1)}, bf16[64,2,4,2,32]{0,4,3,2,1:T(8,128)(2,1)S(1)}, u32[]{:S(2)}) copy-start(bf16[64,2,4,2,32]{0,4,3,2,1:T(8,128)(2,1)S(1)} %rev.8) | copy-start | bytes 196612
  68.7 3.6 %copy-start.5 = (f32[4,64,512]{2,1,0:T(8,128)S(1)}, f32[4,64,512]{2,1,0:T(8,128)}, u32[]{:S(2)}) copy-start(f32[4,64,512]{2,1,0:T(8,128)} %fusion.78) | copy-start | bytes 1572868
  68.7 3.6 %copy-start.11 = (bf16[32,4,512]{2,1,0:T(4,128)(2,1)S(1)}, bf16[32,4,512]{2,1,0:T(4,128)(2,1)}, u32[]{:S(2)}) copy-start(bf16[32,4,512]{2,1,0:T(4,128)(2,1)} %reshape_squeeze.58) | copy-start | bytes 393220
  68.7 3.6 %copy-start.22 = (bf16[64,2,2,2,32]{0,4,3,2,1:T(8,128)(2,1)S(1)}, bf16[64,2,2,2,32]{0,4,3,2,1:T(8,128)(2,1)}, u32[]{:S(2)}) copy-start(bf16[64,2,2,2,32]{0,4,3,2,1:T(8,128)(2,1)} %copy-done.21) | copy-start | bytes 98308
  71.0 1.6 %copy-start.25 = (bf16[64,2,1024]{2,1,0:T(2,128)(2,1)S(1)}, bf16[64,2,1024]{2,1,0:T(2,128)(2,1)}, u32[]{:S(2)}) copy-start(bf16[64,2,1024]{2,1,0:T(2,128)(2,1)} %squeeze.88) | copy-start | bytes 786436
  71.0 1.6 %copy-start.34 = (bf16[32,2,1024]{2,1,0:T(2,128)(2,1)S(1)}, bf16[32,2,1024]{2,1,0:T(2,128)(2,1)}, u32[]{:S(2)}) copy-start(bf16[32,2,1024]{2,1,0:T(2,128)(2,1)} %reshape_squeeze.51) | copy-start | bytes 393220
  71.0 1.8 %copy-start.27 = (bf16[64,2,1024]{2,1,0:T(2,128)(2,1)S(1)}, bf16[64,2,1024]{2,1,0:T(2,128)(2,1)}, u32[]{:S(2)}) copy-start(bf16[64,2,1024]{2,1,0:T(2,128)(2,1)} %squeeze.90) | copy-start | bytes 786436
  72.3 0.9 copy-start.33
  72.3 1.1 copy-start.26
  72.3 1.4 %copy-start.12 = (bf16[32,2,1024]{2,1,0:T(2,128)(2,1)S(1)}, bf16[32,2,1024]{2,1,0:T(2,128)(2,1)}, u32[]{:S(2)}) copy-start(bf16[32,2,1024]{2,1,0:T(2,128)(2,1)} %reshape_squeeze.53) | copy-start | bytes 393220
  73.4 1.2 copy-start.4
  73.4 1.2 copy-start.23
  73.4 1.5 %copy-start.31 = (bf16[64,2,32]{0,2,1:T(8,128)(2,1)}, bf16[64,2,32]{0,2,1:T(8,128)(2,1)S(1)}, u32[]{:S(2)}) copy-start(bf16[64,2,32]{0,2,1:T(8,128)(2,1)S(1)} %squeeze.91) | copy-start | bytes 24580
  74.2 1.1 copy-start.9
  74.2 1.1 copy-start.10
  74.2 1.1 copy-start.17
  74.6 1.1 copy-start.20
  74.6 1.1 copy-start.24
  74.6 1.1 copy-start.37
  74.6 1.3 %copy-start.36 = (f32[64,32]{0,1:T(8,128)S(1)}, f32[64,32]{0,1:T(8,128)}, u32[]{:S(2)}) copy-start(f32[64,32]{0,1:T(8,128)} %convolution_bitcast_fusion.2) | copy-start | bytes 24580
  74.6 1.5 %copy-start.8 = (f32[8,64,256]{2,1,0:T(8,128)S(1)}, f32[8,64,256]{2,1,0:T(8,128)}, u32[]{:S(2)}) copy-start(f32[8,64,256]{2,1,0:T(8,128)} %fusion.62) | copy-start | bytes 1572868
  75.6 1.1 copy-start.7
  76.6 0.8 copy-start.32
  76.7 1.0 copy-start.3
  77.0 1.2 copy-start.6
Sparse Core Ops, SparseCore 0:
  9.0 24.8 all-gather.1
  81.8 30.9 reduce-scatter.1
where the time goes:
time: 122 us; the launch traced here: 121 us
  waiting for transfers between devices  40.1 us (33%)
  matrix products  31.9 us (26%)
  local copies, waits for them, and re-layouts  22.2 us (18%)
  between operations  14.7 us (12%)
  blocking collectives  8.16 us (7%)
  other arithmetic  4.16 us (3%)
    reduce_scatter x1, waiting for transfers between devices, shards(): return lax.psum_scatter(summed, 'ang', scatter_dimension=0, tiled=True)  31.1 us
    dot_general x40, matrix products, single(): return jnp.einsum(form, first, second, preferred_element_type=jnp.float32)  26.3 us
    all_gather x1, waiting for transfers between devices, shards(): lax.all_gather(panels, 'ang', axis=2, tiled=True)[0]  8.91 us
    all_gather x1, blocking collectives, shards(): gathered = lax.all_gather(projected[:, None], 'row', axis=1, tiled=True)  8.16 us
    dot_general x4, matrix products, single(): jnp.einsum('aqk,qsw->askw', coefficient, entry_values, preferred_element_...  5.57 us
    unnamed x87, local copies, waits for them, and re-layouts  5.45 us
    squeeze x2, local copies, waits for them, and re-layouts, near_field(): node_view[:, 1]  2.85 us
  transfers between devices with their start and end apart: 2, of which 2 were waited for; matrix products, arithmetic and copies ran while one was open for 13% of the time, Pallas kernels for 0%

commit v1 on v0

--- a/solution.py
+++ b/solution.py
@@ -2,6 +2,18 @@
 import jax.numpy as jnp
 from jax import lax
 from jax.sharding import PartitionSpec as P
+
+
+def gather_by_bits(x, axis, dim):
+    ways, here, lap = (lax.axis_size(axis), lax.axis_index(axis), x.shape[dim])
+    line, have = (x, 1)
+    while have < ways:
+        line = jnp.concatenate(
+            [line, lax.ppermute(line, axis, [(d, (d - have) % ways) for d in range(ways)])],
+            axis=dim,
+        )
+        have = 2 * have
+    return jnp.roll(line, here * lap, axis=dim)
 
 
 def complex_product(form, left_real, left_imag, right_real, right_imag):
@@ -100,9 +112,7 @@
     theta = own_wave[:, 0:1] * cell_float[None, :, 0] + own_wave[:, 1:2] * cell_float[None, :, 1]
     own_cos = jnp.cos(theta).astype(jnp.bfloat16)
     own_sin = jnp.sin(theta).astype(jnp.bfloat16)
-    excitation = assemble(
-        own_cos, own_sin, onehot, lax.all_gather(panels, "ang", axis=2, tiled=True)[0]
-    )
+    excitation = assemble(own_cos, own_sin, onehot, gather_by_bits(panels, "ang", 2)[0])
     rank_width = block_right.shape[2]
     rank_iota = jnp.arange(rank_width, dtype=jnp.int32)
     rank_masks = (rank_iota[None, :] < rank_count).astype(jnp.bfloat16)

time: 122 us -> 162 us (1.33)
  local copies, waits for them, and re-layouts: 22.2 us -> 43.3 us
  waiting for transfers between devices: 40.1 us -> 52.9 us
  starting transfers between devices: 0.04 us -> 5.79 us
  matrix products: 31.9 us -> 29.3 us
  other arithmetic: 4.16 us -> 6.56 us
    ppermute x0 -> x3, waiting for transfers between devices: none -> 21 us  [gather_by_bits(): lax.ppermute(line, axis, [(d, (d - have) % ways) for d in range(ways)])]
    all_gather x1 -> x0, waiting for transfers between devices: 8.91 us -> none  [shards(): lax.all_gather(panels, 'ang', axis=2, tiled=True)[0]]
    unnamed x87 -> x93, local copies, waits for them, and re-layouts: 5.45 us -> 11.8 us
    ppermute x0 -> x3, starting transfers between devices: none -> 5.79 us  [gather_by_bits(): lax.ppermute(line, axis, [(d, (d - have) % ways) for d in range(ways)])]
    dynamic_slice x0 -> x2, local copies, waits for them, and re-layouts: none -> 2.76 us  [gather_by_bits(): return jnp.roll(line, here * lap, axis=dim)]
    dot_general x4, matrix products: 5.57 us -> 3.39 us  [single(): jnp.einsum('aqk,qsw->askw', coefficient, entry_values, preferred_element_...]
    squeeze x2, local copies, waits for them, and re-layouts: 1.56 us -> 3.5 us  [near_field(): node_view[:, 0]]
    another operation x2, local copies, waits for them, and re-layouts: 0.82 us -> 2.61 us  [near_field(): left_factors[tree_level_index, 1].reshape(rank_width, groups, node_size)]
  transfers between devices with their start and end apart: 2 -> 4, of which waited for: 2 -> 2; matrix products, arithmetic and copies ran while one was open for 13% -> 14% of each run, Pallas kernels for 0% -> 0%
where the time goes in v1:
time: 162 us; the launch traced here: 161 us
  waiting for transfers between devices  52.9 us (33%)
  local copies, waits for them, and re-layouts  43.3 us (27%)
  matrix products  29.3 us (18%)
  between operations  14.7 us (9%)
  blocking collectives  8.48 us (5%)
  other arithmetic  6.56 us (4%)
  starting transfers between devices  5.79 us (4%)
    reduce_scatter x1, waiting for transfers between devices, shards(): return lax.psum_scatter(summed, 'ang', scatter_dimension=0, tiled=True)  31.9 us
    dot_general x40, matrix products, single(): return jnp.einsum(form, first, second, preferred_element_type=jnp.float32)  26 us
    ppermute x3, waiting for transfers between devices, gather_by_bits(): lax.ppermute(line, axis, [(d, (d - have) % ways) for d in range(ways)])  21 us
    unnamed x93, local copies, waits for them, and re-layouts  11.8 us
    all_gather x1, blocking collectives, shards(): gathered = lax.all_gather(projected[:, None], 'row', axis=1, tiled=True)  8.48 us
    ppermute x3, starting transfers between devices, gather_by_bits(): lax.ppermute(line, axis, [(d, (d - have) % ways) for d in range(ways)])  5.79 us
    squeeze x2, local copies, waits for them, and re-layouts, near_field(): node_view[:, 0]  3.5 us
    dot_general x4, matrix products, single(): jnp.einsum('aqk,qsw->askw', coefficient, entry_values, preferred_element_...  3.39 us
  transfers between devices with their start and end apart: 4, of which 2 were waited for; matrix products, arithmetic and copies ran while one was open for 14% of the time, Pallas kernels for 0%

profile of v1, /device:TPU:0, one launch (start us, length us, event | category | flops | bytes accessed | tf_op | source)
XLA Modules:
  0.0 161.0 jit_solution(1739651910366405445)
XLA Ops:
  6.5 4.5 %collective-permute-start = (bf16[1,32,8,2,128]{4,3,2,1,0:T(2,128)(2,1)}, bf16[1,32,8,2,128]{4,3,2,1,0:T(2,128)(2,1)S(1)}, u32[]{:S(2)}, u32[]{:S(2)}) collective-permute-start(bf16[1,32,8,2,128]{4,3,2,1,0:T(2,128)(2,1)} %param.12), channel_id=1, source_target_pairs={{0,28},{4,0},{8,4},{12,8},{16,12},{20,16},{24,20},{28,24},{1,29},{... | collective-permute-start | bytes 393224 | tf_op jit(solution)/shard_map/ppermute | solution.py:12
  12.4 2.0 %fusion.122 = (bf16[1,1,32,2048]{3,2,1,0:T(8,128)(2,1)}, bf16[1,1,32,2048]{3,2,1,0:T(8,128)(2,1)S(1)}, bf16[1,1,32,2048]{3,2,1,0:T(8,128)(2,1)S(1)}, bf16[1,1,32...) fusion(bf16[3,2,32,2048]{3,2,1,0:T(8,128)(2,1)} %bitcast.280), kind=kLoop, calls=%fused_computation.185 | loop fusion | bytes 1572864 | tf_op jit(solution)/shard_map/slice | solution.py:69
  16.1 0.9 broadcast_multiply_fusion
  17.0 1.3 convert_bitcast_fusion.1
  19.1 1.0 pad_maximum_fusion.2
  20.1 1.2 collective-permute-start.1
  22.0 1.6 %reshape_squeeze.51 = bf16[32,2,1024]{2,1,0:T(2,128)(2,1)} reshape(bf16[1,1,32,2048]{3,2,1,0:T(8,128)(2,1)} %get-tuple-element.22) | data formatting | bytes 262144 | tf_op jit(solution)/shard_map/reshape;squeeze | solution.py:68
  23.6 1.6 %reshape_squeeze.52 = bf16[32,2,1024]{2,1,0:T(2,128)(2,1)} reshape(bf16[1,1,32,2048]{3,2,1,0:T(8,128)(2,1)} %get-tuple-element.17) | data formatting | bytes 262144 | tf_op jit(solution)/shard_map/reshape;squeeze | solution.py:69
  25.2 1.6 %reshape_squeeze.53 = bf16[32,2,1024]{2,1,0:T(2,128)(2,1)} reshape(bf16[1,1,32,2048]{3,2,1,0:T(8,128)(2,1)} %get-tuple-element.16) | data formatting | bytes 262144 | tf_op jit(solution)/shard_map/reshape;squeeze | solution.py:77
  26.9 1.6 %reshape_squeeze.54 = bf16[32,2,1024]{2,1,0:T(2,128)(2,1)} reshape(bf16[1,1,32,2048]{3,2,1,0:T(8,128)(2,1)} %get-tuple-element.11) | data formatting | bytes 262144 | tf_op jit(solution)/shard_map/reshape;squeeze | solution.py:78
  30.7 1.0 reshape_squeeze.58
  34.3 0.8 reshape_squeeze.63
  37.4 0.9 constant_dynamic-update-slice_fusion.5
  38.4 21.0 %collective-permute-done.2 = bf16[1,32,32,2,128]{4,3,2,1,0:T(2,128)(2,1)S(1)} collective-permute-done((bf16[1,32,32,2,128]{4,3,2,1,0:T(2,128)(2,1)S(1)}, bf16[1,32,32,2,128]{4,3,2,1,0:T(2,128)(2,1)S(1)}, u32[]{:S(2)}, u32[]{:S(2)}) %collective-permute-start.2) | collective-permute-done | bytes 524320 | tf_op jit(solution)/shard_map/ppermute | solution.py:12
  59.3 1.3 constant_dynamic-update-slice_fusion.4
  62.2 0.9 constant_dynamic-update-slice_fusion.1
  63.1 1.3 constant_dynamic-update-slice_fusion
  64.3 2.1 %constant_dynamic-slice_fusion.1 = bf16[1,32,64,2,128]{4,3,2,1,0:T(2,128)(2,1)S(1)} fusion(bf16[1,32,128,2,128]{4,3,2,1,0:T(2,128)(2,1)} %constant_dynamic-update-slice_fusion, s32[]{:T(128)S(6)} %select_n.17), kind=kLoop, calls=%fused_computation.178 | loop fusion | bytes 2097156 | tf_op jit(solution)/shard_map/jit(_roll_dynamic)/dynamic_slice | solution.py:16
  67.1 1.0 fusion.28
  70.0 1.0 squeeze.87
  71.1 2.0 %fusion.10 = bf16[64,128,16]{1,2,0:T(8,128)(2,1)} fusion(f32[64,128,16]{1,2,0:T(8,128)} %fusion.28, bf16[32,64,2,128]{3,0,1,2:T(8,128)(2,1)S(1)} %bitcast.247, s32[32]{0:T(128)S(1)} %bitcast.299, bf16[32]{0:T(256)(128)(2,1)S(1)} %get-tuple-element.5), kind=kOutput, calls=%fused_computation.22 | convolution fusion | flops 8651776 | bytes 1311744 | tf_op jit(solution)/shard_map/aqk,qsw->askw/dot_general | solution.py:37
  73.0 1.8 %squeeze.88 = bf16[64,2,1024]{2,1,0:T(2,128)(2,1)} reshape(bf16[1,64,16,128]{3,2,1,0:T(8,128)(2,1)} %bitcast.257) | data formatting | bytes 524288 | tf_op jit(solution)/shard_map/squeeze | solution.py:71
  74.8 1.0 squeeze.86
  75.8 1.7 %squeeze.94 = bf16[64,4,512]{2,1,0:T(4,128)(2,1)} reshape(bf16[1,64,16,128]{3,2,1,0:T(8,128)(2,1)} %bitcast.259) | data formatting | bytes 524288 | tf_op jit(solution)/shard_map/squeeze | solution.py:71
  77.6 1.8 %squeeze.95 = bf16[64,4,512]{2,1,0:T(4,128)(2,1)} reshape(bf16[1,64,16,128]{3,2,1,0:T(8,128)(2,1)} %bitcast.254) | data formatting | bytes 524288 | tf_op jit(solution)/shard_map/squeeze | solution.py:71
  79.3 1.2 fusion.52
  80.6 0.9 fusion.54
  81.4 0.9 fusion.60
  84.3 1.1 fusion.78
  85.4 1.1 fusion.80
  86.4 1.2 fusion.12
  87.6 1.2 fusion.13
  89.5 0.9 rev.8
  90.5 1.1 fusion.68
  91.6 1.1 fusion.70
  92.7 1.1 fusion.34
  93.8 1.1 fusion.30
  95.4 8.5 %all_gather.3 = bf16[1,4,64,2,32]{2,4,3,0,1:T(8,128)(2,1)S(1)} all-gather(bf16[1,1,64,2,32]{2,4,3,0,1:T(8,128)(2,1)S(1)} %maximum_bitcast_fusion), channel_id=1, replica_groups=mesh['ang'=8,'row'=4] {'row'}, dimensions={1}, use_global_device_ids=true | all-gather | bytes 40960 | tf_op jit(solution)/shard_map/all_gather | solution.py:129
  104.7 0.8 convolution_bitcast_fusion.2
  106.8 1.2 fusion.19
  108.6 1.0 fusion.88
  109.6 1.0 fusion.90
  110.6 1.0 fusion.6
  111.6 1.5 fusion.2
  117.9 1.6 %subtract_bitcast_fusion = (f32[64,1,2048]{2,0,1:T(8,128)S(1)}, f32[64,1,2048]{2,0,1:T(8,128)S(1)}) fusion(f32[64,2048]{1,0:T(8,128)S(1)} %fusion, f32[]{:T(128)} %bitcast.62, f32[]{:T(128)} %bitcast, f32[64,2048]{1,0:T(8,128)S(1)} %fusion.64, bf16[64,32]{0,1:T(8,128)(2,1)S(1)} %fusion.23, bf16[1,2,32,2048]{3,2,1,0:T(8,128)(2,1)S(1)} %copy-done.4, ...), kind=kOutput, calls=%fused_computation.58 | convolution fusion | flops 9830400 | bytes 4333576 | tf_op jit(solution)/shard_map/rm,sr->sm/dot_general | solution.py:22
  119.6 1.1 pad_maximum_fusion
  120.7 31.9 %reduce-scatter.2.cloned.1.call-done = f32[8,2,2048]{2,0,1:T(8,128)} async-done(((f32[64,2,2048]{2,0,1:T(8,128)}), f32[8,2,2048]{2,0,1:T(8,128)}) %reduce-scatter.2.cloned.1.call-update) | async-done | bytes 131088 | tf_op jit(solution)/shard_map/reduce_scatter | solution.py:159
  152.5 1.7 %copy.140 = f32[8,2,2048]{2,1,0:T(2,128)} copy(f32[8,2,2048]{2,0,1:T(8,128)} %reduce-scatter.2.cloned.1.call-done) | data formatting | bytes 262144 | tf_op jit(solution)/shard_map/reduce_scatter | solution.py:159
  (150 shorter events, 25.4 us)
Async XLA Ops:
  6.5 4.5 %copy-start = (f32[8,2]{0,1:T(2,128)S(1)}, f32[8,2]{0,1:T(2,128)}, u32[]{:S(2)}) copy-start(f32[8,2]{0,1:T(2,128)} %param.15) | copy-start | bytes 196
  6.5 7.8 %copy-start.17 = (bf16[1,3,2,32,2048]{4,3,2,1,0:T(8,128)(2,1)S(1)}, bf16[1,3,2,32,2048]{4,3,2,1,0:T(8,128)(2,1)}, u32[]{:S(2)}) copy-start(bf16[1,3,2,32,2048]{4,3,2,1,0:T(8,128)(2,1)} %param.17) | copy-start | bytes 2359300
  6.5 146.0 %reduce-scatter.2.cloned.1.call-start = ((), (), s32[]{:S(2)}) async-start(), calls=%async_computation.1 | async-start | bytes 1179648 | tf_op jit(solution)/shard_map/reduce_scatter | solution.py:159
  6.5 12.5 %collective-permute-start = (bf16[1,32,8,2,128]{4,3,2,1,0:T(2,128)(2,1)}, bf16[1,32,8,2,128]{4,3,2,1,0:T(2,128)(2,1)S(1)}, u32[]{:S(2)}, u32[]{:S(2)}) collective-permute-start(bf16[1,32,8,2,128]{4,3,2,1,0:T(2,128)(2,1)} %param.12), channel_id=1, source_target_pairs={{0,28},{4,0},{8,4},{12,8},{16,12},{20,16},{24,20},{28,24},{1,29},{... | collective-permute-start | bytes 393224 | tf_op jit(solution)/shard_map/ppermute | solution.py:12
  11.0 4.1 %copy-start.6 = (bf16[1,2,2048,256]{3,2,1,0:T(8,128)(2,1)S(1)}, bf16[1,2,2048,256]{3,2,1,0:T(8,128)(2,1)}, u32[]{:S(2)}) copy-start(bf16[1,2,2048,256]{3,2,1,0:T(8,128)(2,1)} %param.16) | copy-start | bytes 6291460
  15.1 1.0 copy-start.28
  15.1 1.0 copy-start.29
  15.1 3.2 %copy-start.9 = (bf16[1,32,8,2,128]{4,3,2,1,0:T(2,128)(2,1)S(1)}, bf16[1,32,8,2,128]{4,3,2,1,0:T(2,128)(2,1)}, u32[]{:S(2)}) copy-start(bf16[1,32,8,2,128]{4,3,2,1,0:T(2,128)(2,1)} %param.12) | copy-start | bytes 393220
  15.1 6.3 %copy-start.40 = (f32[1,2]{1,0:T(1,128)S(1)}, f32[1,2]{1,0:T(1,128)}, u32[]{:S(2)}) copy-start(f32[1,2]{1,0:T(1,128)} %param.23) | copy-start | bytes 28
  20.1 15.0 %collective-permute-start.1 = (bf16[1,32,16,2,128]{4,3,2,1,0:T(2,128)(2,1)}, bf16[1,32,16,2,128]{4,3,2,1,0:T(2,128)(2,1)S(1)}, u32[]{:S(2)}, u32[]{:S(2)}) collective-permute-start(bf16[1,32,16,2,128]{4,3,2,1,0:T(2,128)(2,1)} %pad_maximum_fusion.2), channel_id=1, source_target_pairs={{0,24},{4,28},{8,0},{12,4},{16,8},{20,12},{24,16},{28,20},{1,25},{... | collective-permute-start | bytes 786440 | tf_op jit(solution)/shard_map/ppermute | solution.py:12
  35.9 23.4 %collective-permute-start.2 = (bf16[1,32,32,2,128]{4,3,2,1,0:T(2,128)(2,1)S(1)}, bf16[1,32,32,2,128]{4,3,2,1,0:T(2,128)(2,1)S(1)}, u32[]{:S(2)}, u32[]{:S(2)}) collective-permute-start(bf16[1,32,32,2,128]{4,3,2,1,0:T(2,128)(2,1)S(1)} %pad_maximum_fusion.1), channel_id=1, source_target_pairs={{0,16},{4,20},{8,24},{12,28},{16,0},{20,4},{24,8},{28,12},{1,17},{... | collective-permute-start | bytes 1572872 | tf_op jit(solution)/shard_map/ppermute | solution.py:12
  64.3 2.8 %copy-start.39 = (s32[1,32]{1,0:T(1,128)S(1)}, s32[1,32]{1,0:T(1,128)}, u32[]{:S(2)}) copy-start(s32[1,32]{1,0:T(1,128)} %param.13) | copy-start | bytes 388
  68.6 0.7 copy-start.1
  73.0 7.5 %copy-start.36 = (bf16[4,8,8,256]{3,2,1,0:T(8,128)(2,1)S(1)}, bf16[4,8,8,256]{3,2,1,0:T(8,128)(2,1)}, u32[]{:S(2)}) copy-start(bf16[4,8,8,256]{3,2,1,0:T(8,128)(2,1)} %copy.151) | copy-start | bytes 393220
  79.3 3.4 %copy-start.26 = (bf16[64,4,512]{2,1,0:T(4,128)(2,1)S(1)}, bf16[64,4,512]{2,1,0:T(4,128)(2,1)}, u32[]{:S(2)}) copy-start(bf16[64,4,512]{2,1,0:T(4,128)(2,1)} %squeeze.94) | copy-start | bytes 786436
  79.3 3.4 %copy-start.35 = (bf16[32,4,512]{2,1,0:T(4,128)(2,1)S(1)}, bf16[32,4,512]{2,1,0:T(4,128)(2,1)}, u32[]{:S(2)}) copy-start(bf16[32,4,512]{2,1,0:T(4,128)(2,1)} %reshape_squeeze.55) | copy-start | bytes 393220
  80.6 2.4 %copy-start.27 = (bf16[64,4,512]{2,1,0:T(4,128)(2,1)S(1)}, bf16[64,4,512]{2,1,0:T(4,128)(2,1)}, u32[]{:S(2)}) copy-start(bf16[64,4,512]{2,1,0:T(4,128)(2,1)} %squeeze.95) | copy-start | bytes 786436
  80.6 2.6 %copy-start.34 = (bf16[32,4,512]{2,1,0:T(4,128)(2,1)S(1)}, bf16[32,4,512]{2,1,0:T(4,128)(2,1)}, u32[]{:S(2)}) copy-start(bf16[32,4,512]{2,1,0:T(4,128)(2,1)} %reshape_squeeze.56) | copy-start | bytes 393220
  82.3 2.0 %copy-start.14 = (bf16[32,4,512]{2,1,0:T(4,128)(2,1)S(1)}, bf16[32,4,512]{2,1,0:T(4,128)(2,1)}, u32[]{:S(2)}) copy-start(bf16[32,4,512]{2,1,0:T(4,128)(2,1)} %reshape_squeeze.57) | copy-start | bytes 393220
  83.4 7.1 %copy-start.13 = (bf16[4,8,8,256]{3,2,1,0:T(8,128)(2,1)S(1)}, bf16[4,8,8,256]{3,2,1,0:T(8,128)(2,1)}, u32[]{:S(2)}) copy-start(bf16[4,8,8,256]{3,2,1,0:T(8,128)(2,1)} %copy.153) | copy-start | bytes 393220
  83.7 0.6 copy-start.20
  84.3 8.4 %copy-start.3 = (bf16[64,128,16]{1,2,0:T(8,128)(2,1)S(1)}, bf16[64,128,16]{1,2,0:T(8,128)(2,1)}, u32[]{:S(2)}) copy-start(bf16[64,128,16]{1,2,0:T(8,128)(2,1)} %fusion.10) | copy-start | bytes 786436
  85.4 8.4 %copy-start.2 = (bf16[64,128,16]{1,2,0:T(8,128)(2,1)S(1)}, bf16[64,128,16]{1,2,0:T(8,128)(2,1)}, u32[]{:S(2)}) copy-start(bf16[64,128,16]{1,2,0:T(8,128)(2,1)} %copy-done.1) | copy-start | bytes 786436
  90.4 2.3 %copy-start.15 = (bf16[64,2,4,2,32]{0,4,3,2,1:T(8,128)(2,1)}, bf16[64,2,4,2,32]{0,4,3,2,1:T(8,128)(2,1)S(1)}, u32[]{:S(2)}) copy-start(bf16[64,2,4,2,32]{0,4,3,2,1:T(8,128)(2,1)S(1)} %rev.8) | copy-start | bytes 196612
  90.4 4.5 %copy-start.30 = (bf16[1,2,32,2048]{3,2,1,0:T(8,128)(2,1)S(1)}, bf16[1,2,32,2048]{3,2,1,0:T(8,128)(2,1)}, u32[]{:S(2)}) copy-start(bf16[1,2,32,2048]{3,2,1,0:T(8,128)(2,1)} %get-tuple-element.30) | copy-start | bytes 786436
  90.4 13.5 %copy-start.22 = (bf16[1,1,32,4,32]{4,3,2,1,0:T(4,128)(2,1)S(1)}, bf16[1,1,32,4,32]{4,3,2,1,0:T(4,128)(2,1)}, u32[]{:S(2)}) copy-start(bf16[1,1,32,4,32]{4,3,2,1,0:T(4,128)(2,1)} %get-tuple-element.24) | copy-start | bytes 24580
  90.4 15.1 %copy-start.24 = (bf16[64,2,1024]{2,1,0:T(2,128)(2,1)S(1)}, bf16[64,2,1024]{2,1,0:T(2,128)(2,1)}, u32[]{:S(2)}) copy-start(bf16[64,2,1024]{2,1,0:T(2,128)(2,1)} %squeeze.90) | copy-start | bytes 786436
  90.4 15.1 %copy-start.33 = (bf16[32,2,1024]{2,1,0:T(2,128)(2,1)S(1)}, bf16[32,2,1024]{2,1,0:T(2,128)(2,1)}, u32[]{:S(2)}) copy-start(bf16[32,2,1024]{2,1,0:T(2,128)(2,1)} %reshape_squeeze.51) | copy-start | bytes 393220
  90.4 15.3 %copy-start.25 = (bf16[64,2,1024]{2,1,0:T(2,128)(2,1)S(1)}, bf16[64,2,1024]{2,1,0:T(2,128)(2,1)}, u32[]{:S(2)}) copy-start(bf16[64,2,1024]{2,1,0:T(2,128)(2,1)} %squeeze.88) | copy-start | bytes 786436
  91.6 14.4 %copy-start.32 = (bf16[32,2,1024]{2,1,0:T(2,128)(2,1)S(1)}, bf16[32,2,1024]{2,1,0:T(2,128)(2,1)}, u32[]{:S(2)}) copy-start(bf16[32,2,1024]{2,1,0:T(2,128)(2,1)} %reshape_squeeze.52) | copy-start | bytes 393220
  93.8 14.8 %copy-start.12 = (bf16[32,2,1024]{2,1,0:T(2,128)(2,1)S(1)}, bf16[32,2,1024]{2,1,0:T(2,128)(2,1)}, u32[]{:S(2)}) copy-start(bf16[32,2,1024]{2,1,0:T(2,128)(2,1)} %reshape_squeeze.53) | copy-start | bytes 393220
  95.1 15.4 %copy-start.10 = (bf16[32,2,1024]{2,1,0:T(2,128)(2,1)S(1)}, bf16[32,2,1024]{2,1,0:T(2,128)(2,1)}, u32[]{:S(2)}) copy-start(bf16[32,2,1024]{2,1,0:T(2,128)(2,1)} %reshape_squeeze.54) | copy-start | bytes 393220
  103.9 4.0 %copy-start.18 = (bf16[1,4,64,2,32]{2,4,1,3,0:T(8,128)(2,1)}, bf16[1,4,64,2,32]{2,4,1,3,0:T(8,128)(2,1)S(1)}, u32[]{:S(2)}) copy-start(bf16[1,4,64,2,32]{2,4,1,3,0:T(8,128)(2,1)S(1)} %copy_multiply_fusion) | copy-start | bytes 98308
  111.5 1.7 %copy-start.5 = (f32[4,64,512]{2,1,0:T(8,128)S(1)}, f32[4,64,512]{2,1,0:T(8,128)}, u32[]{:S(2)}) copy-start(f32[4,64,512]{2,1,0:T(8,128)} %fusion.78) | copy-start | bytes 1572868
  111.6 1.7 %copy-start.21 = (bf16[64,2,2,2,32]{0,4,3,2,1:T(8,128)(2,1)S(1)}, bf16[64,2,2,2,32]{0,4,3,2,1:T(8,128)(2,1)}, u32[]{:S(2)}) copy-start(bf16[64,2,2,2,32]{0,4,3,2,1:T(8,128)(2,1)} %copy-done.20) | copy-start | bytes 98308
  113.1 1.0 copy-start.8
  113.2 1.1 copy-start.11
  113.2 1.1 copy-start.16
  113.2 1.3 copy-start.31
  115.4 1.0 copy-start.7
  115.4 1.3 copy-start.19
  115.4 1.3 copy-start.23
  115.4 1.3 copy-start.38
  115.4 1.5 copy-start.37
  115.4 1.7 %copy-start.4 = (bf16[1,2,32,2048]{3,2,1,0:T(8,128)(2,1)S(1)}, bf16[1,2,32,2048]{3,2,1,0:T(8,128)(2,1)}, u32[]{:S(2)}) copy-start(bf16[1,2,32,2048]{3,2,1,0:T(8,128)(2,1)} %get-tuple-element.29) | copy-start | bytes 786436
Sparse Core Ops, SparseCore 0:
  120.8 31.7 reduce-scatter.1
